TPU v7x, 128 devices: a whole 4x4x4 slice. The times are simulated.
128 devices in a mesh: ctx: 16 (over z_lo, y, core), ch: 8 (over z_hi, x).
Axes of the slice: x: 4, y: 4, z: 4 (z_hi: 2, z_lo: 2; z = z_hi * 2 + z_lo), core: 2. Of those that a mesh axis runs over, the one named last changes fastest.
Arguments:
- inputs: bfloat16 [512, 512, 1024], P('ctx', None, 'ch'), may hold values from -600 to 600
- norm_gain: float32 [1024], P('ch'), may hold values from 0.1 to 1.9
- conv_taps: float32 [2, 3, 1024], P(None, None, 'ch'), may hold values from -3 to 3
- factor_one: bfloat16 [512, 512], replicated, may hold values from -0.25 to 0.25
- factor_two: bfloat16 [512, 512], replicated, may hold values from -0.25 to 0.25
- kernel: bfloat16 [512, 512, 1024], P(None, 'ctx', 'ch'), may hold values from -5 to 5
- grad_out: bfloat16 [512, 512, 1024], P('ctx', None, 'ch'), may hold values from -5 to 5
Outputs:
- input_grad: bfloat16 [512, 512, 1024], P('ctx', None, 'ch')
- kernel_grad: bfloat16 [512, 512, 1024], P(None, 'ctx', 'ch')
- factor_one_grad: float32 [512, 512], replicated
- factor_two_grad: float32 [512, 512], replicated
- gain_grad: float32 [1024], P('ch')
- taps_grad: float32 [2, 3, 1024], P(None, None, 'ch')
All inputs are finite; a program needn't handle non-finite values.
Results may differ from a plain program's by a relative error of at most 0.0081.
Values may be sent and summed in bfloat16 or wider, within the bound.
No kernel may reach another device: no remote copies, remote signals or barrier semaphores. Data moves between devices by JAX's collectives and lax.ppermute only.
A program may use at most 192 MiB of HBM per device.

v0:
```python
import math
import jax
import jax.numpy as jnp
from jax import lax
from jax.sharding import PartitionSpec as P

OUTER = 512
INNER = 512
WIDTH = 1024


def shifted(value, axis, steps):
    count = lax.axis_size(axis)
    initial, last = (max(0, -steps), min(count, count - steps))
    return lax.ppermute(value, axis, [(source, source + steps) for source in range(initial, last)])


def tree_psum(value, axis):
    count = lax.axis_size(axis)
    step = 1
    while step < count:
        pairs = [(source, source ^ step) for source in range(count)]
        value = jax.tree.map(lambda v, r: v + r, value, lax.ppermute(value, axis, pairs))
        step *= 2
    return value


def on_device(inputs, norm_gain, conv_taps, factor_one, factor_two, kernel, grad_out):
    local_outer, inner, chans = inputs.shape
    rows = local_outer * inner
    taps_count = conv_taps.shape[1]
    flat_in = inputs.reshape(rows, chans).astype(jnp.float32)
    squares = tree_psum(jnp.sum(flat_in * flat_in, axis=1), "ch")
    inverse = lax.rsqrt(squares / WIDTH + 1e-05)
    hat = flat_in * inverse[:, None]
    normed = (hat * norm_gain).astype(jnp.bfloat16)
    earlier = shifted(normed[rows - (taps_count - 1) :], "ctx", 1)
    extended = jnp.concatenate([earlier, normed], 0)
    value_pre = jnp.zeros((rows, chans), jnp.float32)
    gate_pre = jnp.zeros((rows, chans), jnp.float32)
    for offset in range(taps_count):
        window = extended[taps_count - 1 - offset : taps_count - 1 - offset + rows]
        value_pre = value_pre + conv_taps[0, offset] * window
        gate_pre = gate_pre + conv_taps[1, offset] * window
    mixed_in = value_pre.astype(jnp.bfloat16).reshape(local_outer, inner, chans)
    gate = jax.nn.sigmoid(gate_pre)
    cotangent = grad_out.reshape(rows, chans).astype(jnp.float32)
    section_one = jnp.einsum(
        "ijc,jk->ikc", mixed_in, factor_one, preferred_element_type=jnp.float32
    ).astype(jnp.bfloat16)
    out_grad = (cotangent * gate).astype(jnp.bfloat16).reshape(local_outer, inner, chans)
    columns = lax.all_to_all(section_one, "ctx", split_axis=1, concat_axis=0, tiled=True)
    kern = kernel.astype(jnp.float32)
    spectrum = (columns.astype(jnp.float32) * kern).astype(jnp.bfloat16)
    section_two = jnp.einsum(
        "ijc,ik->kjc", spectrum, factor_two, preferred_element_type=jnp.float32
    ).astype(jnp.bfloat16)
    back_rows = lax.all_to_all(section_two, "ctx", split_axis=0, concat_axis=1, tiled=True)
    grad_columns = lax.all_to_all(out_grad, "ctx", split_axis=1, concat_axis=0, tiled=True)
    grad_spec = jnp.einsum(
        "kjc,ik->ijc", grad_columns, factor_two, preferred_element_type=jnp.float32
    )
    kernel_grad = (grad_spec * columns.astype(jnp.float32)).astype(jnp.bfloat16)
    grad_section = (grad_spec * kern).astype(jnp.bfloat16)
    two_part = jnp.einsum("ijc,kjc->ik", spectrum, grad_columns, preferred_element_type=jnp.float32)
    two_total = lax.psum(two_part, ("ctx", "ch"))
    grad_rows = lax.all_to_all(grad_section, "ctx", split_axis=0, concat_axis=1, tiled=True)
    back_flat = back_rows.reshape(rows, chans).astype(jnp.float32)
    grad_gate_pre = cotangent * back_flat * gate * (1.0 - gate)
    grad_mixed = jnp.einsum(
        "ikc,jk->ijc", grad_rows, factor_one, preferred_element_type=jnp.float32
    ).reshape(rows, chans)
    one_part = jnp.einsum("ijc,ikc->jk", mixed_in, grad_rows, preferred_element_type=jnp.float32)
    two_total, one_part = lax.optimization_barrier((two_total, one_part))
    one_total = lax.psum(one_part, ("ctx", "ch"))
    later_value, later_gate = shifted(
        (grad_mixed[: taps_count - 1], grad_gate_pre[: taps_count - 1]), "ctx", -1
    )
    ext_value = jnp.concatenate([grad_mixed, later_value], 0)
    ext_gate = jnp.concatenate([grad_gate_pre, later_gate], 0)
    grad_normed = jnp.zeros((rows, chans), jnp.float32)
    value_taps = []
    gate_taps = []
    for offset in range(taps_count):
        grad_normed = grad_normed + conv_taps[0, offset] * ext_value[offset : offset + rows]
        grad_normed = grad_normed + conv_taps[1, offset] * ext_gate[offset : offset + rows]
        window = extended[taps_count - 1 - offset : taps_count - 1 - offset + rows]
        value_taps.append(jnp.sum(grad_mixed * window, axis=0))
        gate_taps.append(jnp.sum(grad_gate_pre * window, axis=0))
    tap_part = jnp.stack([jnp.stack(value_taps), jnp.stack(gate_taps)])
    gain_part = jnp.sum(grad_normed * hat, axis=0)
    gain_total, taps_total = tree_psum((gain_part, tap_part), "ctx")
    scaled = grad_normed * norm_gain
    row_mean = tree_psum(jnp.sum(scaled * hat, axis=1), "ch") / WIDTH
    input_grad = (
        (inverse[:, None] * (scaled - hat * row_mean[:, None]))
        .astype(jnp.bfloat16)
        .reshape(local_outer, inner, chans)
    )
    seq_scale = 1.0 / math.sqrt(OUTER * INNER)
    factor_one_grad = one_total / math.sqrt(OUTER * WIDTH)
    factor_two_grad = two_total / math.sqrt(INNER * WIDTH)
    return (
        input_grad,
        kernel_grad,
        factor_one_grad,
        factor_two_grad,
        gain_total * seq_scale,
        taps_total * seq_scale,
    )


def solution(mesh):
    in_specs = (
        P("ctx", None, "ch"),
        P("ch"),
        P(None, None, "ch"),
        P(),
        P(),
        P(None, "ctx", "ch"),
        P("ctx", None, "ch"),
    )
    out_specs = (P("ctx", None, "ch"), P(None, "ctx", "ch"), P(), P(), P("ch"), P(None, None, "ch"))
    return jax.shard_map(
        on_device, mesh=mesh, in_specs=in_specs, out_specs=out_specs, check_vma=False
    )
```

profile of v0, /device:TPU:1, one launch (start us, length us, event | category | flops | bytes accessed | tf_op | source)
XLA Modules:
  0.0 703.5 jit_solution(7908504238556587428)
XLA Ops:
  7.2 6.5 copy.43
  29.2 7.1 %copy.44 = f32[32,512,128]{2,1,0:T(8,128)} copy(bf16[32,512,128]{1,2,0:T(8,128)(2,1)} %copy.43) | data formatting | bytes 12582912 | tf_op jit(solution)/shard_map/convert_element_type | solution.py:32
  36.3 5.5 multiply_convert_fusion.2
  41.8 6.3 collective-permute-start.3
  48.9 6.5 fusion.10
  60.4 4.5 convert_bitcast_fusion.3
  64.9 8.0 %copy.55 = bf16[32,512,128]{2,0,1:T(8,128)(2,1)} copy(bf16[32,512,128]{1,2,0:T(8,128)(2,1)} %convert_bitcast_fusion.3) | data formatting | bytes 8388608 | tf_op jit(solution)/shard_map/convert_element_type | solution.py:50
  72.9 6.4 all-to-all-start.2
  79.2 6.9 copy.45
  86.1 48.8 %all-to-all-done.2 = bf16[32,512,128]{2,0,1:T(8,128)(2,1)} async-done(((bf16[32,512,128]{2,0,1:T(8,128)(2,1)}), bf16[32,512,128]{2,0,1:T(8,128)(2,1)}, u32[]{:S(2)}, u32[]{:S(2)}) %all-to-all-start.2) | async-done | bytes 4194336 | tf_op jit(solution)/shard_map/all_to_all | solution.py:52
  134.9 4.9 all-to-all-start
  139.8 7.5 %copy.49 = bf16[512,32,128]{0,2,1:T(8,128)(2,1)} copy(bf16[512,32,128]{2,1,0:T(8,128)(2,1)} %param.12) | data formatting | bytes 8388608 | tf_op args[5]
  156.6 9.9 %copy.58 = f32[512,32,128]{0,2,1:T(8,128)} copy(f32[512,32,128]{2,1,0:T(8,128)} %bitcast.104) | data formatting | bytes 16777216 | tf_op jit(solution)/shard_map/convert_element_type | solution.py:54
  166.6 8.9 %convert_bitcast_fusion.2 = bf16[512,32,128]{0,2,1:T(8,128)(2,1)} fusion(bf16[512,512]{1,0:T(8,128)(2,1)S(1)} %copy-done, f32[512,32,128]{0,2,1:T(8,128)} %copy.58, bf16[512,32,128]{0,2,1:T(8,128)(2,1)} %copy.49), kind=kOutput, calls=%fused_computation.66 | convolution fusion | flops 2155872256 | bytes 17301504 | tf_op jit(solution)/shard_map/ijc,ik->kjc/dot_general | solution.py:55
  175.5 7.9 %copy.59 = bf16[512,32,128]{2,1,0:T(8,128)(2,1)} copy(bf16[512,32,128]{0,2,1:T(8,128)(2,1)} %convert_bitcast_fusion.2) | data formatting | bytes 8388608 | tf_op jit(solution)/shard_map/convert_element_type | solution.py:57
  183.4 12.1 %all-to-all-done = bf16[32,512,128]{2,0,1:T(8,128)(2,1)} async-done(((bf16[32,512,128]{2,0,1:T(8,128)(2,1)}), bf16[32,512,128]{2,0,1:T(8,128)(2,1)}, u32[]{:S(2)}, u32[]{:S(2)}) %all-to-all-start) | async-done | bytes 4194336 | tf_op jit(solution)/shard_map/all_to_all | solution.py:59
  195.5 5.1 all-to-all-start.3
  204.8 12.5 %fusion.29 = (bf16[512,32,128]{0,2,1:T(8,128)(2,1)}, bf16[512,32,128]{0,2,1:T(8,128)(2,1)}) fusion(f32[512,32,128]{0,2,1:T(8,128)} %copy.58, bf16[512,32,128]{0,2,1:T(8,128)(2,1)S(1)} %copy-done.3, bf16[512,512]{1,0:T(8,128)(2,1)S(1)} %copy-done, bf16[512,32,128]{2,1,0:T(8,128)(2,1)S(1)} %bitcast.102), kind=kOutput, calls=%fused_computation.53 | convolution fusion | flops 2157969408 | bytes 25690112 | tf_op jit(solution)/shard_map/kjc,ik->ijc/dot_general | solution.py:60
  217.3 7.9 %copy.50 = bf16[512,32,128]{2,1,0:T(8,128)(2,1)} copy(bf16[512,32,128]{0,2,1:T(8,128)(2,1)} %get-tuple-element.42) | data formatting | bytes 8388608 | tf_op jit(solution)/shard_map/convert_element_type | solution.py:64
  225.2 31.3 %all-to-all-done.3 = bf16[512,32,128]{2,1,0:T(8,128)(2,1)} async-done(((bf16[512,32,128]{2,1,0:T(8,128)(2,1)}), bf16[512,32,128]{2,1,0:T(8,128)(2,1)}, u32[]{:S(2)}, u32[]{:S(2)}) %all-to-all-start.3) | async-done | bytes 4194336 | tf_op jit(solution)/shard_map/all_to_all | solution.py:58
  256.5 4.9 all-to-all-start.1
  269.5 47.6 %all-to-all-done.1 = bf16[512,32,128]{2,1,0:T(8,128)(2,1)} async-done(((bf16[512,32,128]{2,1,0:T(8,128)(2,1)}), bf16[512,32,128]{2,1,0:T(8,128)(2,1)}, u32[]{:S(2)}, u32[]{:S(2)}) %all-to-all-start.1) | async-done | bytes 4194336 | tf_op jit(solution)/shard_map/all_to_all | solution.py:67
  320.7 7.0 multiply_reduce_fusion
  327.7 9.0 %copy.53 = f32[32,512,128]{2,1,0:T(8,128)} copy(f32[32,512,128]{1,2,0:T(8,128)} %get-tuple-element.50) | data formatting | bytes 16777216 | tf_op jit(solution)/shard_map/ikc,jk->ijc/transpose | solution.py:70
  337.3 14.0 %fusion.22 = (f32[128]{0:T(128)S(1)}, f32[128]{0:T(128)S(1)}, f32[128]{0:T(128)S(1)}, f32[128]{0:T(128)S(1)}, f32[128]{0:T(128)S(1)}, /*index=5*/f32[16384,128]{1,0:T(8,128)S(1)}) fusion(bf16[16384,128]{1,0:T(8,128)(2,1)} %copy-done.4, bf16[2,128]{1,0:T(2,128)(2,1)S(1)} %collective-permute-done.3, bf16[16384,128]{1,0:T(8,128)(2,1)} %copy-done.7, ...), kind=kLoop, calls=%fused_computation.41 | loop fusion | flops 60816768 | bytes 37753344 | tf_op jit(solution)/shard_map/reduce_sum | solution.py:89
  359.2 24.3 %multiply_reduce_fusion.1 = (f32[128]{0:T(128)S(1)}, f32[16384]{0:T(1024)S(1)}, f32[16384,128]{1,0:T(8,128)}) fusion(f32[32,512,128]{2,1,0:T(8,128)} %copy.44, f32[16384]{0:T(1024)S(1)} %add_rsqrt_fusion, f32[128]{0:T(128)S(1)} %copy-done.13, f32[2,128]{1,0:T(2,128)S(1)} %collective-permute-done.5, f32[16384,128]{1,0:T(8,128)} %copy-done.8, ...), kind=kLoop, calls=%fused_computation.57 | loop fusion | flops 44023680 | bytes 33691648 | tf_op jit(solution)/shard_map/reduce_sum | solution.py:91
  386.7 8.7 %fusion.35 = f32[512,512]{1,0:T(8,128)} fusion(bf16[512,32,128]{2,1,0:T(8,128)(2,1)} %bitcast.103, f32[512,32,128]{0,2,1:T(8,128)S(1)} %bitcast.99, bf16[512,32,128]{0,2,1:T(8,128)(2,1)} %copy.49), kind=kOutput, calls=%fused_computation.73 | convolution fusion | flops 2153775104 | bytes 17825792 | tf_op jit(solution)/shard_map/ijc,kjc->ik/dot_general | solution.py:65
  395.4 7.9 %copy.64 = bf16[512,32,128]{2,1,0:T(8,128)(2,1)} copy(bf16[512,32,128]{0,2,1:T(8,128)(2,1)} %get-tuple-element.41) | data formatting | bytes 8388608
  404.7 6.8 convolution_bitcast_fusion.1
  411.6 130.2 %all-reduce.3.cloned.1.call-done = f32[512,512]{1,0:T(8,128)} async-done(((f32[512,512]{1,0:T(8,128)}), f32[512,512]{1,0:T(8,128)}) %all-reduce.3.cloned.1.call-update) | async-done | bytes 1048592 | tf_op jit(solution)/shard_map/psum | solution.py:66
  557.9 11.5 %multiply_convert_fusion.1 = bf16[16384,128]{1,0:T(8,128)(2,1)} fusion(f32[16384,128]{1,0:T(8,128)} %get-tuple-element.38, f32[32,512,128]{2,1,0:T(8,128)} %copy.44, f32[16384]{0:T(1024)S(1)} %add_multiply_fusion, f32[128]{0:T(128)S(1)} %copy-done.13, f32[16384]{0:T(1024)S(1)} %add_rsqrt_fusion), kind=kLoop, calls=%fused_computation.58 | loop fusion | flops 12582912 | bytes 21103104 | tf_op jit(solution)/shard_map/convert_element_type | solution.py:97
  569.5 124.7 %all-reduce.5.cloned.1.call-done = f32[512,512]{1,0:T(8,128)} async-done(((f32[512,512]{1,0:T(8,128)}), f32[512,512]{1,0:T(8,128)}) %all-reduce.5.cloned.1.call-update) | async-done | bytes 1048592 | tf_op jit(solution)/shard_map/psum | solution.py:75
  (106 shorter events, 77.9 us)
Async XLA Ops:
  7.2 159.4 %copy-start = (bf16[512,512]{1,0:T(8,128)(2,1)S(1)}, bf16[512,512]{1,0:T(8,128)(2,1)}, u32[]{:S(2)}) copy-start(bf16[512,512]{1,0:T(8,128)(2,1)} %param.11) | copy-start | bytes 1572868
  13.7 22.7 %copy-start.13 = (f32[128]{0:T(128)S(1)}, f32[128]{0:T(128)}, u32[]{:S(2)}) copy-start(f32[128]{0:T(128)} %param.8) | copy-start | bytes 1540
  16.8 3.8 collective-permute-start
  20.6 4.7 collective-permute-start.1
  25.3 11.0 %collective-permute-start.2 = (f32[16384]{0:T(1024)S(1)}, f32[16384]{0:T(1024)S(1)}, u32[]{:S(2)}, u32[]{:S(2)}) collective-permute-start(f32[16384]{0:T(1024)S(1)} %add.83), channel_id=1, source_target_pairs={{0,4},{1,5},{2,6},{3,7},{4,0},{5,1},{6,2},{7,3},{8,12},{9,13},{10,... | collective-permute-start | bytes 196616 | tf_op jit(solution)/shard_map/ppermute | solution.py:23
  36.3 12.6 %copy-start.10 = (bf16[32,512,128]{2,1,0:T(8,128)(2,1)S(1)}, bf16[32,512,128]{2,1,0:T(8,128)(2,1)}, u32[]{:S(2)}) copy-start(bf16[32,512,128]{2,1,0:T(8,128)(2,1)} %param.13) | copy-start | bytes 12582916
  41.8 13.6 %copy-start.4 = (bf16[16384,128]{1,0:T(8,128)(2,1)}, bf16[16384,128]{1,0:T(8,128)(2,1)S(1)}, u32[]{:S(2)}) copy-start(bf16[16384,128]{1,0:T(8,128)(2,1)S(1)} %multiply_convert_fusion.2) | copy-start | bytes 12582916
  41.8 7.1 %collective-permute-start.3 = (bf16[2,128]{1,0:T(2,128)(2,1)S(1)}, bf16[2,128]{1,0:T(2,128)(2,1)S(1)}, u32[]{:S(2)}, u32[]{:S(2)}) collective-permute-start(bf16[2,128]{1,0:T(2,128)(2,1)S(1)} %slice.68), channel_id=1, source_target_pairs={{0,8},{8,16},{16,24},{24,32},{32,40},{40,48},{48,56},{56,64},{64,7... | collective-permute-start | bytes 1544 | tf_op jit(solution)/shard_map/ppermute | solution.py:15
  72.9 62.0 %all-to-all-start.2 = ((bf16[32,512,128]{2,0,1:T(8,128)(2,1)}), bf16[32,512,128]{2,0,1:T(8,128)(2,1)}, u32[]{:S(2)}, u32[]{:S(2)}) async-start(bf16[32,512,128]{2,0,1:T(8,128)(2,1)} %copy.55), calls=%async_computation.2 | async-start | bytes 8388608 | tf_op jit(solution)/shard_map/all_to_all | solution.py:52
  134.9 60.6 %all-to-all-start = ((bf16[32,512,128]{2,0,1:T(8,128)(2,1)}), bf16[32,512,128]{2,0,1:T(8,128)(2,1)}, u32[]{:S(2)}, u32[]{:S(2)}) async-start(bf16[32,512,128]{2,0,1:T(8,128)(2,1)} %copy.45), calls=%async_computation | async-start | bytes 8388608 | tf_op jit(solution)/shard_map/all_to_all | solution.py:59
  195.5 61.0 %all-to-all-start.3 = ((bf16[512,32,128]{2,1,0:T(8,128)(2,1)}), bf16[512,32,128]{2,1,0:T(8,128)(2,1)}, u32[]{:S(2)}, u32[]{:S(2)}) async-start(bf16[512,32,128]{2,1,0:T(8,128)(2,1)} %copy.59), calls=%async_computation.3 | async-start | bytes 8388608 | tf_op jit(solution)/shard_map/all_to_all | solution.py:58
  204.7 12.6 %copy-start.5 = (bf16[16,32,32,128]{3,2,1,0:T(8,128)(2,1)}, bf16[16,32,32,128]{3,2,1,0:T(8,128)(2,1)S(1)}, u32[]{:S(2)}) copy-start(bf16[16,32,32,128]{3,2,1,0:T(8,128)(2,1)S(1)} %copy.47) | copy-start | bytes 12582916
  256.5 60.6 %all-to-all-start.1 = ((bf16[512,32,128]{2,1,0:T(8,128)(2,1)}), bf16[512,32,128]{2,1,0:T(8,128)(2,1)}, u32[]{:S(2)}, u32[]{:S(2)}) async-start(bf16[512,32,128]{2,1,0:T(8,128)(2,1)} %copy.50), calls=%async_computation.1 | async-start | bytes 8388608 | tf_op jit(solution)/shard_map/all_to_all | solution.py:67
  261.4 280.4 %all-reduce.3.cloned.1.call-start = ((), (), s32[]{:S(2)}) async-start(), calls=%async_computation.4 | async-start | bytes 2097152 | tf_op jit(solution)/shard_map/psum | solution.py:66
  337.3 21.9 %copy-start.2 = (f32[32,512,128]{2,1,0:T(8,128)S(1)}, f32[32,512,128]{2,1,0:T(8,128)}, u32[]{:S(2)}) copy-start(f32[32,512,128]{2,1,0:T(8,128)} %copy.53) | copy-start | bytes 25165828
  351.3 5.9 collective-permute-start.5
  353.9 5.3 collective-permute-start.4
  355.9 30.8 %slice-start = ((s8[8388608]{0:T(1024)(128)(4,1)}), s8[4194304]{0:T(1024)(128)(4,1)S(1)}, s32[]{:S(2)}) async-start(s8[8388608]{0:T(1024)(128)(4,1)} %bitcast.98), calls=%async_computation.6 | async-start | bytes 8388608
  355.9 30.8 %slice-start.1 = ((s8[8388608]{0:T(1024)(128)(4,1)}), s8[4194304]{0:T(1024)(128)(4,1)S(1)}, s32[]{:S(2)}) async-start(s8[8388608]{0:T(1024)(128)(4,1)} %bitcast.98), calls=%async_computation.7 | async-start | bytes 8388608
  383.5 1.2 collective-permute-start.9
  383.6 21.1 %collective-permute-start.13 = (f32[2,3,128]{2,1,0:T(4,128)S(1)}, f32[2,3,128]{2,1,0:T(4,128)S(1)}, u32[]{:S(2)}, u32[]{:S(2)}) collective-permute-start(f32[2,3,128]{2,1,0:T(4,128)S(1)} %pad_maximum_fusion.3), channel_id=1, source_target_pairs={{0,8},{8,0},{16,24},{24,16},{32,40},{40,32},{48,56},{56,48},{64,72... | collective-permute-start | bytes 9224 | tf_op jit(solution)/shard_map/ppermute | solution.py:23
  384.7 18.6 %collective-permute-start.10 = (f32[128]{0:T(128)S(1)}, f32[128]{0:T(128)S(1)}, u32[]{:S(2)}, u32[]{:S(2)}) collective-permute-start(f32[128]{0:T(128)S(1)} %add.100), channel_id=1, source_target_pairs={{0,16},{8,24},{16,0},{24,8},{32,48},{40,56},{48,32},{56,40},{64,80... | collective-permute-start | bytes 1544 | tf_op jit(solution)/shard_map/ppermute | solution.py:23
  395.4 298.7 %all-reduce.5.cloned.1.call-start = ((), (), s32[]{:S(2)}) async-start(), calls=%async_computation.5 | async-start | bytes 2097152 | tf_op jit(solution)/shard_map/psum | solution.py:75
  403.3 138.9 %collective-permute-start.11 = (f32[128]{0:T(128)S(1)}, f32[128]{0:T(128)S(1)}, u32[]{:S(2)}, u32[]{:S(2)}) collective-permute-start(f32[128]{0:T(128)S(1)} %add.101), channel_id=1, source_target_pairs={{0,32},{8,40},{16,48},{24,56},{32,0},{40,8},{48,16},{56,24},{64,96... | collective-permute-start | bytes 1544 | tf_op jit(solution)/shard_map/ppermute | solution.py:23
  404.6 138.4 %collective-permute-start.14 = (f32[2,3,128]{2,1,0:T(4,128)S(1)}, f32[2,3,128]{2,1,0:T(4,128)S(1)}, u32[]{:S(2)}, u32[]{:S(2)}) collective-permute-start(f32[2,3,128]{2,1,0:T(4,128)S(1)} %fusion.42), channel_id=1, source_target_pairs={{0,16},{8,24},{16,0},{24,8},{32,48},{40,56},{48,32},{56,40},{64,80... | collective-permute-start | bytes 9224 | tf_op jit(solution)/shard_map/ppermute | solution.py:23
  541.7 6.5 collective-permute-start.6
  542.2 8.1 %collective-permute-start.12 = (f32[128]{0:T(128)S(1)}, f32[128]{0:T(128)S(1)}, u32[]{:S(2)}, u32[]{:S(2)}) collective-permute-start(f32[128]{0:T(128)S(1)} %add.102), channel_id=1, source_target_pairs={{0,64},{8,72},{16,80},{24,88},{32,96},{40,104},{48,112},{56,120},{... | collective-permute-start | bytes 1544 | tf_op jit(solution)/shard_map/ppermute | solution.py:23
  543.1 4.0 collective-permute-start.15
  547.1 8.2 %collective-permute-start.16 = (f32[2,3,128]{2,1,0:T(4,128)S(1)}, f32[2,3,128]{2,1,0:T(4,128)S(1)}, u32[]{:S(2)}, u32[]{:S(2)}) collective-permute-start(f32[2,3,128]{2,1,0:T(4,128)S(1)} %add.106), channel_id=1, source_target_pairs={{0,64},{8,72},{16,80},{24,88},{32,96},{40,104},{48,112},{56,120},{... | collective-permute-start | bytes 9224 | tf_op jit(solution)/shard_map/ppermute | solution.py:23
  548.2 4.7 collective-permute-start.7
  552.9 5.0 collective-permute-start.8
  557.9 138.5 %copy-start.1 = (bf16[512,512]{1,0:T(8,128)(2,1)S(1)}, bf16[512,512]{1,0:T(8,128)(2,1)}, u32[]{:S(2)}) copy-start(bf16[512,512]{1,0:T(8,128)(2,1)} %param.11) | copy-start | bytes 1572868
  (8 other events, 41.2 us)
Sparse Core Ops, SparseCore 0:
  395.5 146.1 all-reduce.2
  547.1 147.0 all-reduce.4
where the time goes:
time: 712 us; the launch traced here: 703 us
  waiting for transfers between devices  407 us (57%)
  local copies, waits for them, and re-layouts  102 us (14%)
  other arithmetic  77.7 us (11%)
  starting transfers between devices  54 us (8%)
  matrix products  48.5 us (7%)
  between operations  14.6 us (2%)
    psum x1, waiting for transfers between devices, on_device(): two_total = lax.psum(two_part, ('ctx', 'ch'))  130 us
    psum x1, waiting for transfers between devices, on_device(): one_total = lax.psum(one_part, ('ctx', 'ch'))  125 us
    all_to_all x1, waiting for transfers between devices, on_device(): lax.all_to_all(section_one, 'ctx', split_axis=1, concat_axis=0, tiled=True)  48.8 us
    all_to_all x1, waiting for transfers between devices, on_device(): lax.all_to_all(grad_section, 'ctx', split_axis=0, concat_axis=1, tiled=True)  47.6 us
    all_to_all x1, waiting for transfers between devices, on_device(): lax.all_to_all(section_two, 'ctx', split_axis=0, concat_axis=1, tiled=True)  31.3 us
    unnamed x39, local copies, waits for them, and re-layouts  24.5 us
    reduce_sum x1, other arithmetic, on_device(): gain_part = jnp.sum(grad_normed * hat, axis=0)  24.3 us
    ppermute x14, starting transfers between devices, tree_psum(): lax.ppermute(value, axis, pairs)  21.5 us
  transfers between devices with their start and end apart: 23, of which 15 were waited for; matrix products, arithmetic and copies ran while one was open for 18% of the time, Pallas kernels for 0%

commit v1 on v0

--- a/solution.py
+++ b/solution.py
@@ -64,7 +64,9 @@
     grad_section = (grad_spec * kern).astype(jnp.bfloat16)
     two_part = jnp.einsum("ijc,kjc->ik", spectrum, grad_columns, preferred_element_type=jnp.float32)
     two_total = lax.psum(two_part, ("ctx", "ch"))
-    grad_rows = lax.all_to_all(grad_section, "ctx", split_axis=0, concat_axis=1, tiled=True)
+    pieces = jnp.split(grad_section, lax.axis_size("ctx"), axis=0)
+    received = lax.all_to_all(jnp.stack(pieces), "ctx", 0, 0)
+    grad_rows = jnp.concatenate(received, axis=1)
     back_flat = back_rows.reshape(rows, chans).astype(jnp.float32)
     grad_gate_pre = cotangent * back_flat * gate * (1.0 - gate)
     grad_mixed = jnp.einsum(

time: 712 us -> 735 us (1.032)
  local copies, waits for them, and re-layouts: 102 us -> 154 us
  waiting for transfers between devices: 407 us -> 376 us
    another operation x0 -> x18, local copies, waits for them, and re-layouts: none -> 39.9 us  [on_device(): received = lax.all_to_all(jnp.stack(pieces), 'ctx', 0, 0)]
    all_to_all x1, waiting for transfers between devices: 31.3 us -> 0.01 us  [on_device(): lax.all_to_all(section_two, 'ctx', split_axis=0, concat_axis=1, tiled=True)]
    unnamed x39 -> x56, local copies, waits for them, and re-layouts: 24.5 us -> 44.9 us
    convert_element_type x1 -> x0, local copies, waits for them, and re-layouts: 7.89 us -> none  [on_device(): grad_section = (grad_spec * kern).astype(jnp.bfloat16)]
  transfers between devices with their start and end apart: 23 -> 23, of which waited for: 15 -> 14; matrix products, arithmetic and copies ran while one was open for 18% -> 25% of each run, Pallas kernels for 0% -> 0%
where the time goes in v1:
time: 735 us; the launch traced here: 725 us
  waiting for transfers between devices  376 us (51%)
  local copies, waits for them, and re-layouts  154 us (21%)
  other arithmetic  77.8 us (11%)
  starting transfers between devices  54.9 us (7%)
  matrix products  47.9 us (7%)
  between operations  14.7 us (2%)
    psum x1, waiting for transfers between devices, on_device(): two_total = lax.psum(two_part, ('ctx', 'ch'))  130 us
    psum x1, waiting for transfers between devices, on_device(): one_total = lax.psum(one_part, ('ctx', 'ch'))  125 us
    all_to_all x1, waiting for transfers between devices, on_device(): lax.all_to_all(section_one, 'ctx', split_axis=1, concat_axis=0, tiled=True)  48.8 us
    all_to_all x1, waiting for transfers between devices, on_device(): received = lax.all_to_all(jnp.stack(pieces), 'ctx', 0, 0)  47.9 us
    unnamed x56, local copies, waits for them, and re-layouts  44.9 us
    another operation x18, local copies, waits for them, and re-layouts, on_device(): received = lax.all_to_all(jnp.stack(pieces), 'ctx', 0, 0)  39.9 us
    reduce_sum x1, other arithmetic, on_device(): gain_part = jnp.sum(grad_normed * hat, axis=0)  24.4 us
    ppermute x14, starting transfers between devices, tree_psum(): lax.ppermute(value, axis, pairs)  21.5 us
  transfers between devices with their start and end apart: 23, of which 14 were waited for; matrix products, arithmetic and copies ran while one was open for 25% of the time, Pallas kernels for 0%

profile of v1, /device:TPU:1, one launch (start us, length us, event | category | flops | bytes accessed | tf_op | source)
XLA Modules:
  0.0 725.4 jit_solution(7383191246290707501)
XLA Ops:
  7.2 6.5 copy.80
  29.2 7.1 copy.81
  36.4 5.5 multiply_convert_fusion.2
  41.9 6.3 collective-permute-start.3
  48.9 6.5 fusion.10
  60.4 4.5 convert_bitcast_fusion.3
  64.9 8.0 %copy.107 = bf16[32,512,128]{2,0,1:T(8,128)(2,1)} copy(bf16[32,512,128]{1,2,0:T(8,128)(2,1)} %convert_bitcast_fusion.3) | data formatting | bytes 8388608 | tf_op jit(solution)/shard_map/convert_element_type | solution.py:50
  72.9 6.3 all-to-all-start.2
  79.3 6.9 copy.82
  86.2 48.8 %all-to-all-done.2 = bf16[32,512,128]{2,0,1:T(8,128)(2,1)} async-done(((bf16[32,512,128]{2,0,1:T(8,128)(2,1)}), bf16[32,512,128]{2,0,1:T(8,128)(2,1)}, u32[]{:S(2)}, u32[]{:S(2)}) %all-to-all-start.2) | async-done | bytes 4194336 | tf_op jit(solution)/shard_map/all_to_all | solution.py:52
  135.0 4.9 all-to-all-start
  139.8 7.6 %copy.86 = bf16[512,32,128]{0,2,1:T(8,128)(2,1)} copy(bf16[512,32,128]{2,1,0:T(8,128)(2,1)} %param.12) | data formatting | bytes 8388608 | tf_op args[5]
  152.4 4.3 copy.109
  156.7 10.0 %copy.110 = f32[512,32,128]{0,2,1:T(8,128)} copy(f32[512,32,128]{2,1,0:T(8,128)} %bitcast.135) | data formatting | bytes 16777216 | tf_op jit(solution)/shard_map/convert_element_type | solution.py:54
  166.7 8.9 %convert_bitcast_fusion.2 = bf16[512,32,128]{0,2,1:T(8,128)(2,1)} fusion(bf16[512,512]{1,0:T(8,128)(2,1)S(1)} %copy-done, f32[512,32,128]{0,2,1:T(8,128)} %copy.110, bf16[512,32,128]{0,2,1:T(8,128)(2,1)} %copy.86), kind=kOutput, calls=%fused_computation.66 | convolution fusion | flops 2155872256 | bytes 17301504 | tf_op jit(solution)/shard_map/ijc,ik->kjc/dot_general | solution.py:55
  175.6 7.9 %copy.111 = bf16[512,32,128]{2,1,0:T(8,128)(2,1)} copy(bf16[512,32,128]{0,2,1:T(8,128)(2,1)} %convert_bitcast_fusion.2) | data formatting | bytes 8388608 | tf_op jit(solution)/shard_map/convert_element_type | solution.py:57
  183.5 12.0 %all-to-all-done = bf16[32,512,128]{2,0,1:T(8,128)(2,1)} async-done(((bf16[32,512,128]{2,0,1:T(8,128)(2,1)}), bf16[32,512,128]{2,0,1:T(8,128)(2,1)}, u32[]{:S(2)}, u32[]{:S(2)}) %all-to-all-start) | async-done | bytes 4194336 | tf_op jit(solution)/shard_map/all_to_all | solution.py:59
  195.6 5.5 all-to-all-start.3
  205.2 11.9 %fusion.29 = (bf16[512,32,128]{0,2,1:T(8,128)(2,1)}, bf16[512,32,128]{0,2,1:T(8,128)(2,1)S(1)}) fusion(f32[512,32,128]{0,2,1:T(8,128)} %copy.110, bf16[512,32,128]{0,2,1:T(8,128)(2,1)S(1)} %copy-done.3, bf16[512,512]{1,0:T(8,128)(2,1)S(1)} %copy-done, bf16[512,32,128]{2,1,0:T(8,128)(2,1)S(1)} %bitcast.133), kind=kOutput, calls=%fused_computation.53 | convolution fusion | flops 2157969408 | bytes 25690112 | tf_op jit(solution)/shard_map/kjc,ik->ijc/dot_general | solution.py:60
  217.1 7.6 %slice_bitcast_fusion = (bf16[1,32,32,128]{1,3,2,0:T(8,128)(2,1)}, bf16[1,32,32,128]{1,3,2,0:T(8,128)(2,1)}, bf16[1,32,32,128]{1,3,2,0:T(8,128)(2,1)}, bf16[1,32...) fusion(bf16[512,32,128]{0,2,1:T(8,128)(2,1)S(1)} %get-tuple-ele, ...), kind=kLoop, calls=%fused_computation.75 | loop fusion | bytes 8388608 | tf_op jit(solution)/shard_map/stack | solution.py:68
  277.5 5.7 all-to-all-start.1
  291.1 47.9 %all-to-all-done.1 = bf16[16,32,32,128]{3,2,1,0:T(8,128)(2,1)} async-done(((bf16[16,32,32,128]{3,2,1,0:T(8,128)(2,1)}), bf16[16,32,32,128]{3,2,1,0:T(8,128)(2,1)}, u32[]{:S(2)}, u32[]{:S(2)}) %all-to-all-start.1) | async-done | bytes 4194336 | tf_op jit(solution)/shard_map/all_to_all | solution.py:68
  342.6 7.0 multiply_reduce_fusion
  349.7 9.0 %copy.105 = f32[32,512,128]{2,1,0:T(8,128)} copy(f32[32,512,128]{1,2,0:T(8,128)} %get-tuple-element.72) | data formatting | bytes 16777216 | tf_op jit(solution)/shard_map/ikc,jk->ijc/transpose | solution.py:72
  359.3 14.0 %fusion.22 = (f32[128]{0:T(128)S(1)}, f32[128]{0:T(128)S(1)}, f32[128]{0:T(128)S(1)}, f32[128]{0:T(128)S(1)}, f32[128]{0:T(128)S(1)}, /*index=5*/f32[16384,128]{1,0:T(8,128)S(1)}) fusion(bf16[16384,128]{1,0:T(8,128)(2,1)} %copy-done.4, bf16[2,128]{1,0:T(2,128)(2,1)S(1)} %collective-permute-done.3, bf16[16384,128]{1,0:T(8,128)(2,1)} %copy-done.7, ...), kind=kLoop, calls=%fused_computation.41 | loop fusion | flops 60816768 | bytes 37753344 | tf_op jit(solution)/shard_map/reduce_sum | solution.py:91
  381.1 24.4 %multiply_reduce_fusion.1 = (f32[128]{0:T(128)S(1)}, f32[16384]{0:T(1024)S(1)}, f32[16384,128]{1,0:T(8,128)}) fusion(f32[32,512,128]{2,1,0:T(8,128)} %copy.81, f32[16384]{0:T(1024)S(1)} %add_rsqrt_fusion, f32[128]{0:T(128)S(1)} %copy-done.14, f32[2,128]{1,0:T(2,128)S(1)} %collective-permute-done.5, f32[16384,128]{1,0:T(8,128)} %copy-done.8, ...), kind=kLoop, calls=%fused_computation.57 | loop fusion | flops 44023680 | bytes 33691648 | tf_op jit(solution)/shard_map/reduce_sum | solution.py:93
  408.7 8.7 %fusion.35 = f32[512,512]{1,0:T(8,128)} fusion(bf16[512,32,128]{2,1,0:T(8,128)(2,1)} %bitcast.134, f32[512,32,128]{0,2,1:T(8,128)S(1)} %bitcast.130, bf16[512,32,128]{0,2,1:T(8,128)(2,1)} %copy.86), kind=kOutput, calls=%fused_computation.73 | convolution fusion | flops 2153775104 | bytes 17825792 | tf_op jit(solution)/shard_map/ijc,kjc->ik/dot_general | solution.py:65
  417.4 7.9 %copy.116 = bf16[512,32,128]{2,1,0:T(8,128)(2,1)} copy(bf16[512,32,128]{0,2,1:T(8,128)(2,1)} %get-tuple-element.47) | data formatting | bytes 8388608
  426.6 6.8 convolution_bitcast_fusion.1
  433.5 130.1 %all-reduce.3.cloned.1.call-done = f32[512,512]{1,0:T(8,128)} async-done(((f32[512,512]{1,0:T(8,128)}), f32[512,512]{1,0:T(8,128)}) %all-reduce.3.cloned.1.call-update) | async-done | bytes 1048592 | tf_op jit(solution)/shard_map/psum | solution.py:66
  579.8 11.5 %multiply_convert_fusion.1 = bf16[16384,128]{1,0:T(8,128)(2,1)} fusion(f32[16384,128]{1,0:T(8,128)} %get-tuple-element.44, f32[32,512,128]{2,1,0:T(8,128)} %copy.81, f32[16384]{0:T(1024)S(1)} %add_multiply_fusion, f32[128]{0:T(128)S(1)} %copy-done.14, f32[16384]{0:T(1024)S(1)} %add_rsqrt_fusion), kind=kLoop, calls=%fused_computation.58 | loop fusion | flops 12582912 | bytes 21103104 | tf_op jit(solution)/shard_map/convert_element_type | solution.py:99
  591.3 124.7 %all-reduce.5.cloned.1.call-done = f32[512,512]{1,0:T(8,128)} async-done(((f32[512,512]{1,0:T(8,128)}), f32[512,512]{1,0:T(8,128)}) %all-reduce.5.cloned.1.call-update) | async-done | bytes 1048592 | tf_op jit(solution)/shard_map/psum | solution.py:77
  (140 shorter events, 126.0 us)
Async XLA Ops:
  7.2 159.5 %copy-start = (bf16[512,512]{1,0:T(8,128)(2,1)S(1)}, bf16[512,512]{1,0:T(8,128)(2,1)}, u32[]{:S(2)}) copy-start(bf16[512,512]{1,0:T(8,128)(2,1)} %param.11) | copy-start | bytes 1572868
  13.7 22.7 %copy-start.14 = (f32[128]{0:T(128)S(1)}, f32[128]{0:T(128)}, u32[]{:S(2)}) copy-start(f32[128]{0:T(128)} %param.8) | copy-start | bytes 1540
  16.8 3.8 collective-permute-start
  20.6 4.7 collective-permute-start.1
  25.3 11.0 %collective-permute-start.2 = (f32[16384]{0:T(1024)S(1)}, f32[16384]{0:T(1024)S(1)}, u32[]{:S(2)}, u32[]{:S(2)}) collective-permute-start(f32[16384]{0:T(1024)S(1)} %add.83), channel_id=1, source_target_pairs={{0,4},{1,5},{2,6},{3,7},{4,0},{5,1},{6,2},{7,3},{8,12},{9,13},{10,... | collective-permute-start | bytes 196616 | tf_op jit(solution)/shard_map/ppermute | solution.py:23
  36.3 12.6 %copy-start.10 = (bf16[32,512,128]{2,1,0:T(8,128)(2,1)S(1)}, bf16[32,512,128]{2,1,0:T(8,128)(2,1)}, u32[]{:S(2)}) copy-start(bf16[32,512,128]{2,1,0:T(8,128)(2,1)} %param.13) | copy-start | bytes 12582916
  41.8 13.6 %copy-start.4 = (bf16[16384,128]{1,0:T(8,128)(2,1)}, bf16[16384,128]{1,0:T(8,128)(2,1)S(1)}, u32[]{:S(2)}) copy-start(bf16[16384,128]{1,0:T(8,128)(2,1)S(1)} %multiply_convert_fusion.2) | copy-start | bytes 12582916
  41.9 7.1 collective-permute-start.3
  72.9 62.0 %all-to-all-start.2 = ((bf16[32,512,128]{2,0,1:T(8,128)(2,1)}), bf16[32,512,128]{2,0,1:T(8,128)(2,1)}, u32[]{:S(2)}, u32[]{:S(2)}) async-start(bf16[32,512,128]{2,0,1:T(8,128)(2,1)} %copy.107), calls=%async_computation.2 | async-start | bytes 8388608 | tf_op jit(solution)/shard_map/all_to_all | solution.py:52
  135.0 60.6 %all-to-all-start = ((bf16[32,512,128]{2,0,1:T(8,128)(2,1)}), bf16[32,512,128]{2,0,1:T(8,128)(2,1)}, u32[]{:S(2)}, u32[]{:S(2)}) async-start(bf16[32,512,128]{2,0,1:T(8,128)(2,1)} %copy.82), calls=%async_computation | async-start | bytes 8388608 | tf_op jit(solution)/shard_map/all_to_all | solution.py:59
  195.6 81.9 %all-to-all-start.3 = ((bf16[512,32,128]{2,1,0:T(8,128)(2,1)}), bf16[512,32,128]{2,1,0:T(8,128)(2,1)}, u32[]{:S(2)}, u32[]{:S(2)}) async-start(bf16[512,32,128]{2,1,0:T(8,128)(2,1)} %copy.111), calls=%async_computation.3 | async-start | bytes 8388608 | tf_op jit(solution)/shard_map/all_to_all | solution.py:58
  277.5 61.6 %all-to-all-start.1 = ((bf16[16,32,32,128]{3,2,1,0:T(8,128)(2,1)}), bf16[16,32,32,128]{3,2,1,0:T(8,128)(2,1)}, u32[]{:S(2)}, u32[]{:S(2)}) async-start(bf16[16,32,32,128]{3,2,1,0:T(8,128)(2,1)} %constant_dynamic-update-slice_fusion), calls=%async_computation.1 | async-start | bytes 8388608 | tf_op jit(solution)/shard_map/all_to_all | solution.py:68
  283.2 280.4 %all-reduce.3.cloned.1.call-start = ((), (), s32[]{:S(2)}) async-start(), calls=%async_computation.4 | async-start | bytes 2097152 | tf_op jit(solution)/shard_map/psum | solution.py:66
  291.1 51.5 %copy-start.13 = (bf16[512,512]{1,0:T(8,128)(2,1)S(1)}, bf16[512,512]{1,0:T(8,128)(2,1)}, u32[]{:S(2)}) copy-start(bf16[512,512]{1,0:T(8,128)(2,1)} %param.10) | copy-start | bytes 1572868
  359.3 21.7 %copy-start.2 = (f32[32,512,128]{2,1,0:T(8,128)S(1)}, f32[32,512,128]{2,1,0:T(8,128)}, u32[]{:S(2)}) copy-start(f32[32,512,128]{2,1,0:T(8,128)} %copy.105) | copy-start | bytes 25165828
  373.3 5.8 collective-permute-start.5
  375.8 5.3 collective-permute-start.4
  377.8 30.9 %slice-start = ((s8[8388608]{0:T(1024)(128)(4,1)}), s8[4194304]{0:T(1024)(128)(4,1)S(1)}, s32[]{:S(2)}) async-start(s8[8388608]{0:T(1024)(128)(4,1)} %bitcast.129), calls=%async_computation.6 | async-start | bytes 8388608
  377.8 30.9 %slice-start.1 = ((s8[8388608]{0:T(1024)(128)(4,1)}), s8[4194304]{0:T(1024)(128)(4,1)S(1)}, s32[]{:S(2)}) async-start(s8[8388608]{0:T(1024)(128)(4,1)} %bitcast.129), calls=%async_computation.7 | async-start | bytes 8388608
  405.5 1.2 collective-permute-start.9
  405.5 21.1 %collective-permute-start.13 = (f32[2,3,128]{2,1,0:T(4,128)S(1)}, f32[2,3,128]{2,1,0:T(4,128)S(1)}, u32[]{:S(2)}, u32[]{:S(2)}) collective-permute-start(f32[2,3,128]{2,1,0:T(4,128)S(1)} %pad_maximum_fusion.3), channel_id=1, source_target_pairs={{0,8},{8,0},{16,24},{24,16},{32,40},{40,32},{48,56},{56,48},{64,72... | collective-permute-start | bytes 9224 | tf_op jit(solution)/shard_map/ppermute | solution.py:23
  406.6 18.7 %collective-permute-start.10 = (f32[128]{0:T(128)S(1)}, f32[128]{0:T(128)S(1)}, u32[]{:S(2)}, u32[]{:S(2)}) collective-permute-start(f32[128]{0:T(128)S(1)} %add.100), channel_id=1, source_target_pairs={{0,16},{8,24},{16,0},{24,8},{32,48},{40,56},{48,32},{56,40},{64,80... | collective-permute-start | bytes 1544 | tf_op jit(solution)/shard_map/ppermute | solution.py:23
  417.4 298.6 %all-reduce.5.cloned.1.call-start = ((), (), s32[]{:S(2)}) async-start(), calls=%async_computation.5 | async-start | bytes 2097152 | tf_op jit(solution)/shard_map/psum | solution.py:77
  425.3 138.7 %collective-permute-start.11 = (f32[128]{0:T(128)S(1)}, f32[128]{0:T(128)S(1)}, u32[]{:S(2)}, u32[]{:S(2)}) collective-permute-start(f32[128]{0:T(128)S(1)} %add.101), channel_id=1, source_target_pairs={{0,32},{8,40},{16,48},{24,56},{32,0},{40,8},{48,16},{56,24},{64,96... | collective-permute-start | bytes 1544 | tf_op jit(solution)/shard_map/ppermute | solution.py:23
  426.5 138.4 %collective-permute-start.14 = (f32[2,3,128]{2,1,0:T(4,128)S(1)}, f32[2,3,128]{2,1,0:T(4,128)S(1)}, u32[]{:S(2)}, u32[]{:S(2)}) collective-permute-start(f32[2,3,128]{2,1,0:T(4,128)S(1)} %fusion.42), channel_id=1, source_target_pairs={{0,16},{8,24},{16,0},{24,8},{32,48},{40,56},{48,32},{56,40},{64,80... | collective-permute-start | bytes 9224 | tf_op jit(solution)/shard_map/ppermute | solution.py:23
  563.6 6.5 collective-permute-start.6
  564.1 8.1 %collective-permute-start.12 = (f32[128]{0:T(128)S(1)}, f32[128]{0:T(128)S(1)}, u32[]{:S(2)}, u32[]{:S(2)}) collective-permute-start(f32[128]{0:T(128)S(1)} %add.102), channel_id=1, source_target_pairs={{0,64},{8,72},{16,80},{24,88},{32,96},{40,104},{48,112},{56,120},{... | collective-permute-start | bytes 1544 | tf_op jit(solution)/shard_map/ppermute | solution.py:23
  564.9 4.0 collective-permute-start.15
  569.0 8.2 %collective-permute-start.16 = (f32[2,3,128]{2,1,0:T(4,128)S(1)}, f32[2,3,128]{2,1,0:T(4,128)S(1)}, u32[]{:S(2)}, u32[]{:S(2)}) collective-permute-start(f32[2,3,128]{2,1,0:T(4,128)S(1)} %add.106), channel_id=1, source_target_pairs={{0,64},{8,72},{16,80},{24,88},{32,96},{40,104},{48,112},{56,120},{... | collective-permute-start | bytes 9224 | tf_op jit(solution)/shard_map/ppermute | solution.py:23
  570.1 4.7 collective-permute-start.7
  574.8 5.0 collective-permute-start.8
  579.8 138.5 %copy-start.1 = (bf16[512,512]{1,0:T(8,128)(2,1)S(1)}, bf16[512,512]{1,0:T(8,128)(2,1)}, u32[]{:S(2)}) copy-start(bf16[512,512]{1,0:T(8,128)(2,1)} %param.11) | copy-start | bytes 1572868
  (9 other events, 53.1 us)
Sparse Core Ops, SparseCore 0:
  417.5 146.0 all-reduce.2
  568.9 147.0 all-reduce.4
